TPU v7x, 32 devices: a whole 2x2x4 slice. The times are simulated.
32 devices in a mesh: req: 4 (over y, x), exp: 8 (over z, core).
Axes of the slice: x: 2, y: 2, z: 4, core: 2. Of those that a mesh axis runs over, the one named last changes fastest.
Arguments:
- tokens: bfloat16 [4, 512, 2048], P('req', 'exp'), may hold values from -6 to 6
- cache: bfloat16 [4, 1024, 4096], P('req', None, 'exp'), may hold values from -64 to 64
- cache_len: int32 [4], P('req'), may hold values from 1 to 1024, 2560 in all
- attn_routes: int32 [4, 512, 2], P('req', 'exp'), may hold values from 0 to 7, all different within a row; in each aligned block of 64 rows (0 to 63, 64 to 127, ..., all dimensions but the last counted through in order) at most 24 rows name the same one
- mlp_routes: int32 [4, 512, 2], P('req', 'exp'), may hold values from 0 to 7, all different within a row; in each aligned block of 64 rows (0 to 63, 64 to 127, ..., all dimensions but the last counted through in order) at most 24 rows name the same one
- norm_attn: float32 [2048], replicated, may hold values from 0.5 to 1.5
- attn_router: bfloat16 [2048, 8], replicated, may hold values from -0.125 to 0.125
- w_query: bfloat16 [128, 2048, 128], P('exp'), may hold values from -0.125 to 0.125
- w_keyval: bfloat16 [2048, 4096], P(None, 'exp'), may hold values from -0.125 to 0.125
- w_out: bfloat16 [128, 128, 2048], P('exp'), may hold values from -0.125 to 0.125
- norm_mlp: float32 [2048], replicated, may hold values from 0.5 to 1.5
- mlp_router: bfloat16 [2048, 8], replicated, may hold values from -0.125 to 0.125
- w_gate: bfloat16 [8, 2048, 5632], P('exp'), may hold values from -0.125 to 0.125
- w_up: bfloat16 [8, 2048, 5632], P('exp'), may hold values from -0.125 to 0.125
- w_down: bfloat16 [8, 5632, 2048], P('exp'), may hold values from -0.078125 to 0.078125
Outputs:
- hidden_out: bfloat16 [4, 512, 2048], P('req', 'exp')
- cache_out: bfloat16 [4, 1536, 4096], P('req', None, 'exp')
Inputs may be any that keep to these rules, and one draw needn't show every extreme that they name: `attn_routes`: in each aligned block of 64 rows, no expert is named by more than 24 rows. `mlp_routes`: in each aligned block of 64 rows, no expert is named by more than 24 rows.
All inputs are finite; a program needn't handle non-finite values. No bound on the sum of `cache_len` on one device may be relied on, other than what follows from the above.
Results may differ from a plain program's by a relative error of at most 0.015.
The roundings to bfloat16 on the way count: a program that leaves them out, or rounds other values in their place, can miss the bound.
Values may be sent and summed in bfloat16 or wider, within the bound.
No kernel may reach another device: no remote copies, remote signals or barrier semaphores. Data moves between devices by JAX's collectives and lax.ppermute only.
A program may use at most 256 MiB of HBM per device.

v0:
```python
import functools
import math

import jax
import jax.numpy as jnp
from jax import lax
from jax.experimental import pallas as pl
from jax.experimental.pallas import tpu as pltpu
from jax.sharding import PartitionSpec as P

MOST = 24


epsilon = 1e-05
rope_base = 10000.0
masked_score = -1e30


def from_partner(value, axis, stride):
    mask = 2**stride
    pairs = [(source, source ^ mask) for source in range(lax.axis_size(axis))]
    return lax.ppermute(value, axis, pairs)


def rms_norm(values, gain_vec):
    widened = values.astype(jnp.float32)
    inv_rms = lax.rsqrt(jnp.mean(widened * widened, axis=-1, keepdims=True) + epsilon)
    return (widened * inv_rms * gain_vec).astype(jnp.bfloat16)


def rotate(values, position):
    half_dim = values.shape[-1] // 2
    inv_freq = rope_base ** (-jnp.arange(half_dim).astype(jnp.float32) / half_dim)
    angles = position.astype(jnp.float32)[..., None] * inv_freq
    cosine = jnp.cos(angles)
    sines = jnp.sin(angles)
    first_half = values[..., :half_dim]
    second_half = values[..., half_dim:]
    return jnp.concatenate(
        [first_half * cosine - second_half * sines, second_half * cosine + first_half * sines],
        axis=-1,
    )


def rotate_whole(values, position):
    half_dim = values.shape[-1] // 2
    inv_freq = rope_base ** (-jnp.arange(half_dim).astype(jnp.float32) / half_dim)
    angles = position.astype(jnp.float32)[..., None] * inv_freq
    cosine = jnp.cos(angles)
    sines = jnp.sin(angles)
    swapped = jnp.concatenate([values[..., half_dim:], values[..., :half_dim]], axis=-1)
    return values * jnp.concatenate([cosine, cosine], axis=-1) + swapped * jnp.concatenate(
        [-sines, sines], axis=-1
    )


def pick_gates(normed, router, routes):
    logits = jnp.dot(normed, router, preferred_element_type=jnp.float32)
    labels = jnp.arange(router.shape[1], dtype=jnp.int32)
    onehot = (routes[:, :, None] == labels[None, None, :]).astype(jnp.float32)
    chosen = jnp.sum(onehot * logits[:, None, :], axis=-1)
    return jax.nn.softmax(chosen, axis=-1)


def slot_tables(routes, gates, labels, rows_block, slot_count):
    row_total = routes.shape[0]
    block_count = row_total // rows_block
    matches = routes[:, :, None] == labels[None, None, :]
    member = jnp.any(matches, axis=1).astype(jnp.int32).reshape(block_count, rows_block, -1)
    weight = jnp.sum(jnp.where(matches, gates[:, :, None], 0.0), axis=1).reshape(
        block_count, rows_block, -1
    )
    ranking = jnp.cumsum(member, axis=1) - 1
    slot_ids = jnp.arange(slot_count, dtype=jnp.int32)
    onehot = ((member[..., None] > 0) & (ranking[..., None] == slot_ids)).astype(jnp.int32)
    local_row = jnp.arange(rows_block, dtype=jnp.int32)[None, :, None, None]
    token_ids = (
        jnp.sum(onehot * local_row, axis=1)
        + (jnp.arange(block_count, dtype=jnp.int32) * rows_block)[:, None, None]
    )
    shares = jnp.sum(onehot.astype(jnp.float32) * weight[..., None], axis=1)
    return (token_ids, shares)


def spread_rows(terms, token_ids, extent):
    term_part = terms.reshape(-1, terms.shape[-1])
    id_part = token_ids.reshape(-1)
    return jnp.zeros((extent, terms.shape[-1]), jnp.float32).at[id_part].add(term_part, mode="drop")


def attend(queries, query_pos, key_cache, value_cache, key_fresh, value_fresh, length):
    query_count = queries.shape[0]
    head_dim = queries.shape[1]
    factor = head_dim ** (-0.5)

    def absorb(state, key_block, value_block, visible):
        running_top, running_total, running_acc = state
        scores = jnp.dot(queries, key_block.T, preferred_element_type=jnp.float32) * factor
        scores = jnp.where(visible, scores, masked_score)
        new_top = jnp.maximum(running_top, jnp.max(scores, axis=1))
        fading = jnp.exp(running_top - new_top)
        weights = jnp.exp(scores - new_top[:, None])
        running_total = running_total * fading + jnp.sum(weights, axis=1)
        running_acc = running_acc * fading[:, None] + jnp.dot(
            weights.astype(jnp.bfloat16), value_block, preferred_element_type=jnp.float32
        )
        return (new_top, running_total, running_acc)

    state = (
        jnp.full((query_count,), masked_score, jnp.float32),
        jnp.zeros((query_count,), jnp.float32),
        jnp.zeros((query_count, head_dim), jnp.float32),
    )
    cache_span = math.gcd(512, key_cache.shape[0])

    def cache_step(step_idx, state):
        offset = step_idx * cache_span
        key_block = lax.dynamic_slice_in_dim(key_cache, offset, cache_span, 0)
        value_block = lax.dynamic_slice_in_dim(value_cache, offset, cache_span, 0)
        visible = (offset + jnp.arange(cache_span, dtype=jnp.int32))[None, :] < length
        return absorb(state, key_block, value_block, visible)

    state = lax.fori_loop(0, (length + cache_span - 1) // cache_span, cache_step, state)
    fresh_span = math.gcd(512, key_fresh.shape[0])
    for offset in range(0, key_fresh.shape[0], fresh_span):
        visible = (offset + jnp.arange(fresh_span, dtype=jnp.int32))[None, :] <= query_pos[:, None]
        state = absorb(
            state,
            key_fresh[offset : offset + fresh_span],
            value_fresh[offset : offset + fresh_span],
            visible,
        )
    running_top, running_total, running_acc = state
    return (running_acc / running_total[:, None]).astype(jnp.bfloat16)


def running_count(member):
    rows = member.shape[0]
    lower = (
        jnp.arange(rows, dtype=jnp.int32)[None, :] <= jnp.arange(rows, dtype=jnp.int32)[:, None]
    ).astype(jnp.bfloat16)
    counts = jnp.dot(lower, member.astype(jnp.bfloat16), preferred_element_type=jnp.float32)
    return counts.astype(jnp.int32)


def local_slots(routes, labels, slot_count):
    matches = routes[:, :, None] == labels[None, None, :]
    member = jnp.any(matches, axis=1).astype(jnp.int32)
    ranking = running_count(member) - 1
    slot_ids = jnp.arange(slot_count, dtype=jnp.int32)
    onehot = ((member[..., None] > 0) & (ranking[..., None] == slot_ids)).astype(jnp.int32)
    rows = jnp.arange(routes.shape[0], dtype=jnp.int32)[:, None, None]
    return jnp.sum(onehot * rows, axis=0)


def route_slots(routes, label_count):
    labels = jnp.arange(label_count, dtype=jnp.int32)
    member = jnp.any(routes[:, :, None] == labels[None, None, :], axis=1).astype(jnp.int32)
    ranking = running_count(member) - 1
    return jnp.take_along_axis(ranking, routes, axis=1)


def select_rows(index, source):
    onehot = (index[:, None] == jnp.arange(source.shape[0], dtype=jnp.int32)[None, :]).astype(
        source.dtype
    )
    return jnp.dot(onehot, source, preferred_element_type=jnp.float32)


def combine(received, routes, gates, slots, split_count):
    slot_count = received.shape[1]
    flat = received.reshape(-1, received.shape[-1])
    total = jnp.zeros((routes.shape[0], received.shape[-1]), jnp.float32)
    for route in range(routes.shape[1]):
        expert = routes[:, route]
        part = jnp.zeros_like(total)
        for piece in range(split_count):
            index = (expert * split_count + piece) * slot_count + slots[:, route]
            part = part + lax.optimization_barrier(select_rows(index, flat))
        total = total + part * gates[:, route][:, None]
    return total


def mlp_kernel(x_ref, gate_ref, up_ref, down_ref, out_ref, acc_ref):
    step = pl.program_id(0)

    @pl.when(step == 0)
    def _():
        acc_ref[...] = jnp.zeros_like(acc_ref)

    rows = x_ref[...]
    gate_part = jnp.dot(rows, gate_ref[...], preferred_element_type=jnp.float32)
    up_part = jnp.dot(rows, up_ref[...], preferred_element_type=jnp.float32)
    hidden = (gate_part / (1.0 + jnp.exp(-gate_part)) * up_part).astype(jnp.bfloat16)
    acc_ref[...] += jnp.dot(hidden, down_ref[...], preferred_element_type=jnp.float32)

    @pl.when(step == pl.num_programs(0) - 1)
    def _():
        out_ref[...] = acc_ref[...].astype(out_ref.dtype)


def expert_mlp(rows, w_gate, w_up, w_down):
    row_count, width = rows.shape
    hidden_units = w_gate.shape[-1]
    tile = next(t for t in (1408, 512, 256, 128) if hidden_units % t == 0)
    return pl.pallas_call(
        mlp_kernel,
        grid=(hidden_units // tile,),
        in_specs=[
            pl.BlockSpec((row_count, width), lambda k: (0, 0)),
            pl.BlockSpec((None, width, tile), lambda k: (0, 0, k)),
            pl.BlockSpec((None, width, tile), lambda k: (0, 0, k)),
            pl.BlockSpec((None, tile, width), lambda k: (0, k, 0)),
        ],
        out_specs=pl.BlockSpec((row_count, width), lambda k: (0, 0)),
        out_shape=jax.ShapeDtypeStruct((row_count, width), jnp.bfloat16),
        scratch_shapes=[pltpu.VMEM((row_count, width), jnp.float32)],
        compiler_params=pltpu.CompilerParams(dimension_semantics=("arbitrary",)),
    )(rows, w_gate, w_up, w_down)


def attention_kernel(length_ref, query_ref, pos_ref, key_ref, value_ref, out_ref, *, cache_limit):
    length = length_ref[0]
    queries = query_ref[...]
    factor = queries.shape[-1] ** (-0.5)
    scores = (
        lax.dot_general(
            queries, key_ref[...], (((1,), (1,)), ((), ())), preferred_element_type=jnp.float32
        )
        * factor
    )
    column = lax.broadcasted_iota(jnp.int32, scores.shape, 1)
    in_cache = column < cache_limit
    visible = (in_cache & (column < length)) | (
        jnp.logical_not(in_cache) & (column - cache_limit <= pos_ref[...])
    )
    scores = jnp.where(visible, scores, masked_score)
    top = jnp.max(scores, axis=1, keepdims=True)
    weights = jnp.exp(scores - top)
    total = jnp.sum(weights, axis=1, keepdims=True)
    summed = jnp.dot(weights.astype(jnp.bfloat16), value_ref[...], preferred_element_type=jnp.float32)
    out_ref[...] = (summed / total).astype(out_ref.dtype)


def kernel_attention(queries, query_pos, keys, values, length, cache_limit):
    head_count, query_count, head_dim = queries.shape
    key_count = keys.shape[1]
    tile = next(t for t in (512, 256, 128, 64, 32, 16, 8) if query_count % t == 0)
    grid_spec = pltpu.PrefetchScalarGridSpec(
        num_scalar_prefetch=1,
        grid=(head_count, query_count // tile),
        in_specs=[
            pl.BlockSpec((None, tile, head_dim), lambda h, i, n: (h, i, 0)),
            pl.BlockSpec((tile, 1), lambda h, i, n: (i, 0)),
            pl.BlockSpec((None, key_count, head_dim), lambda h, i, n: (h, 0, 0)),
            pl.BlockSpec((None, key_count, head_dim), lambda h, i, n: (h, 0, 0)),
        ],
        out_specs=pl.BlockSpec((None, tile, head_dim), lambda h, i, n: (h, i, 0)),
    )
    return pl.pallas_call(
        functools.partial(attention_kernel, cache_limit=cache_limit),
        grid_spec=grid_spec,
        out_shape=jax.ShapeDtypeStruct(queries.shape, jnp.bfloat16),
        compiler_params=pltpu.CompilerParams(dimension_semantics=("arbitrary", "arbitrary")),
    )(jnp.reshape(length, (1,)).astype(jnp.int32), queries, query_pos.reshape(-1, 1), keys, values)


def head_attention(queries, query_pos, keys, values, length, cache_limit):
    factor = queries.shape[-1] ** (-0.5)
    scores = jnp.einsum("hqk,hsk->hqs", queries, keys, preferred_element_type=jnp.float32) * factor
    slot_ids = jnp.arange(keys.shape[1], dtype=jnp.int32)[None, :]
    visible = jnp.where(
        slot_ids < cache_limit, slot_ids < length, slot_ids - cache_limit <= query_pos[:, None]
    )
    scores = jnp.where(visible[None], scores, masked_score)
    top = jnp.max(scores, axis=-1, keepdims=True)
    weights = jnp.exp(scores - top)
    total = jnp.sum(weights, axis=-1, keepdims=True)
    summed = jnp.einsum(
        "hqs,hsk->hqk", weights.astype(jnp.bfloat16), values, preferred_element_type=jnp.float32
    )
    return (summed / total).astype(jnp.bfloat16)


def body(
    tokens,
    cache,
    cache_len,
    attn_routes,
    mlp_routes,
    norm_attn,
    attn_router,
    w_query,
    w_keyval,
    w_out,
    norm_mlp,
    mlp_router,
    w_gate,
    w_up,
    w_down,
):
    device_count = lax.axis_size("exp")
    position = lax.axis_index("exp")
    own_rows = tokens[0]
    rows_block = own_rows.shape[0]
    model_width = own_rows.shape[1]
    length = cache_len[0]
    slot_count = MOST
    heads_here = w_query.shape[0]
    head_dim = w_query.shape[2]
    columns = w_keyval.shape[1]
    experts_attn = attn_router.shape[1]
    kv_heads = columns * device_count // (2 * head_dim)
    fast_attn = (
        device_count == experts_attn and heads_here == kv_heads and columns % (2 * head_dim) == 0
    )
    if not fast_attn:
        return base_body(
            tokens, cache, cache_len, attn_routes, mlp_routes, norm_attn, attn_router, w_query,
            w_keyval, w_out, norm_mlp, mlp_router, w_gate, w_up, w_down,
        )
    normed = rms_norm(own_rows, norm_attn)
    route_rows = jnp.zeros((16, 2 * rows_block), jnp.bfloat16)
    route_rows = route_rows.at[0].set(attn_routes[0].reshape(-1).astype(jnp.bfloat16))
    group_normed = lax.all_gather(normed, "exp", axis=0, tiled=True)
    gathered_routes = lax.all_gather(route_rows, "exp", axis=0, tiled=False)
    group_routes = gathered_routes[:, 0].astype(jnp.int32).reshape(-1, 2)
    row_total = group_normed.shape[0]
    block_count = row_total // rows_block
    new_pos = length + jnp.arange(row_total, dtype=jnp.int32)
    fresh_kv = jnp.dot(group_normed, w_keyval, preferred_element_type=jnp.float32)
    split_new = fresh_kv.reshape(row_total, columns // (2 * head_dim), 2, head_dim)
    rotated = rotate(split_new[:, :, 0], new_pos[:, None])
    fresh_kv = (
        jnp.stack([rotated, split_new[:, :, 1]], axis=2)
        .astype(jnp.bfloat16)
        .reshape(row_total, columns)
    )
    cache_limit = cache.shape[1]
    padded = jnp.concatenate([cache[0], jnp.zeros((row_total, columns), jnp.bfloat16)], axis=0)
    placed = lax.dynamic_update_slice(jnp.zeros_like(padded), fresh_kv, (length, jnp.int32(0)))
    slot_ids = jnp.arange(cache_limit + row_total, dtype=jnp.int32)
    cache_next = jnp.where((slot_ids < length)[:, None], padded, placed)

    all_labels = jnp.arange(experts_attn, dtype=jnp.int32)
    blocks_routes = group_routes.reshape(block_count, rows_block, -1)
    slot_tokens = jax.vmap(lambda r: local_slots(r, all_labels, slot_count))(blocks_routes)
    slot_tokens = slot_tokens + (jnp.arange(block_count, dtype=jnp.int32) * rows_block)[:, None, None]
    expert_tokens = jnp.swapaxes(slot_tokens, 0, 1).reshape(experts_attn, -1)
    my_tokens = expert_tokens[position]
    picked_rows = select_rows(my_tokens, group_normed).astype(jnp.bfloat16)
    queries = jnp.einsum("sd,hdk->hsk", picked_rows, w_query, preferred_element_type=jnp.float32)
    queries = rotate_whole(queries, (length + my_tokens)[None, :]).astype(jnp.bfloat16)
    heads_local = columns // (2 * head_dim)
    query_slots = queries.shape[1]
    send_q = queries.reshape(device_count, heads_local, query_slots, head_dim)
    recv_q = lax.all_to_all(send_q, "exp", 0, 0, tiled=True)
    recv_q = jnp.swapaxes(recv_q, 0, 1).reshape(heads_local, device_count * query_slots, head_dim)
    query_pos = expert_tokens.reshape(-1)
    split_old = cache[0].reshape(cache_limit, heads_local, 2, head_dim)
    split_fresh = fresh_kv.reshape(row_total, heads_local, 2, head_dim)
    keys = jnp.swapaxes(jnp.concatenate([split_old[:, :, 0], split_fresh[:, :, 0]], axis=0), 0, 1)
    values = jnp.swapaxes(jnp.concatenate([split_old[:, :, 1], split_fresh[:, :, 1]], axis=0), 0, 1)
    out_by_head = w_out.reshape(device_count, heads_local, head_dim, model_width)
    projected = jnp.zeros((query_slots, model_width), jnp.float32)
    for head in range(heads_local):
        head_out = kernel_attention(
            recv_q[head : head + 1], query_pos, keys[head : head + 1], values[head : head + 1],
            length, cache_limit,
        )
        recv_o = lax.all_to_all(
            head_out.reshape(device_count, query_slots, head_dim), "exp", 0, 0, tiled=True
        )
        projected = projected + jnp.einsum(
            "dsk,dkm->sm", recv_o, out_by_head[:, head], preferred_element_type=jnp.float32
        )
    send_p = projected.astype(jnp.bfloat16).reshape(block_count, slot_count, model_width)
    recv_p = lax.all_to_all(send_p, "exp", 0, 0, tiled=True)
    own_attn_routes = attn_routes[0]
    attn_gates = pick_gates(normed, attn_router, own_attn_routes)
    attn_own = combine(
        recv_p, own_attn_routes, attn_gates, route_slots(own_attn_routes, experts_attn), 1
    )
    middle = (own_rows.astype(jnp.float32) + attn_own).astype(jnp.bfloat16)
    normed_mlp = rms_norm(middle, norm_mlp)
    experts_mlp = mlp_router.shape[1]
    split_count = device_count // experts_mlp
    own_mlp_routes = mlp_routes[0]
    mlp_gates = pick_gates(normed_mlp, mlp_router, own_mlp_routes)
    mlp_tokens = local_slots(own_mlp_routes, jnp.arange(experts_mlp, dtype=jnp.int32), slot_count)
    dest_tokens = jnp.repeat(mlp_tokens, split_count, axis=0)
    send_m = (
        select_rows(dest_tokens.reshape(-1), normed_mlp)
        .astype(jnp.bfloat16)
        .reshape(device_count, slot_count, model_width)
    )
    inputs = lax.all_to_all(send_m, "exp", 0, 0, tiled=True).reshape(-1, model_width)
    slice_out = expert_mlp(inputs, w_gate, w_up, w_down)
    recv_m = lax.all_to_all(
        slice_out.reshape(device_count, slot_count, model_width), "exp", 0, 0, tiled=True
    )
    mlp_own = combine(
        recv_m, own_mlp_routes, mlp_gates, route_slots(own_mlp_routes, experts_mlp), split_count
    )
    layer_out = (middle.astype(jnp.float32) + mlp_own).astype(jnp.bfloat16)
    return (layer_out[None], cache_next[None])


def base_body(
    tokens,
    cache,
    cache_len,
    attn_routes,
    mlp_routes,
    norm_attn,
    attn_router,
    w_query,
    w_keyval,
    w_out,
    norm_mlp,
    mlp_router,
    w_gate,
    w_up,
    w_down,
):
    device_count = lax.axis_size("exp")
    position = lax.axis_index("exp")
    own_rows = tokens[0]
    rows_block = own_rows.shape[0]
    model_width = own_rows.shape[1]
    length = cache_len[0]
    slot_count = MOST
    normed = rms_norm(own_rows, norm_attn)
    group_normed, group_routes = (
        lax.all_gather(normed, "exp", axis=0, tiled=True),
        lax.all_gather(attn_routes[0], "exp", axis=0, tiled=True),
    )
    row_total = group_normed.shape[0]
    block_count = row_total // rows_block
    heads_here = w_query.shape[0]
    head_dim = w_query.shape[2]
    columns = w_keyval.shape[1]
    experts_attn = attn_router.shape[1]
    my_attn = jnp.reshape(position % experts_attn, (1,))
    new_pos = length + jnp.arange(row_total, dtype=jnp.int32)
    fresh_kv = jnp.dot(group_normed, w_keyval, preferred_element_type=jnp.float32)
    if columns < 2 * head_dim:
        is_key = position % 2 == 0
        fresh_kv = jnp.where(is_key, rotate(fresh_kv, new_pos), fresh_kv).astype(jnp.bfloat16)
    else:
        split_new = fresh_kv.reshape(row_total, columns // (2 * head_dim), 2, head_dim)
        rotated = rotate(split_new[:, :, 0], new_pos[:, None])
        fresh_kv = (
            jnp.stack([rotated, split_new[:, :, 1]], axis=2)
            .astype(jnp.bfloat16)
            .reshape(row_total, columns)
        )
    cache_limit = cache.shape[1]
    padded = jnp.concatenate([cache[0], jnp.zeros((row_total, columns), jnp.bfloat16)], axis=0)
    placed = lax.dynamic_update_slice(jnp.zeros_like(padded), fresh_kv, (length, jnp.int32(0)))
    slot_ids = jnp.arange(cache_limit + row_total, dtype=jnp.int32)
    cache_next = jnp.where((slot_ids < length)[:, None], padded, placed)
    group_cache = cache[0]
    group_fresh = fresh_kv
    for bit in range(experts_attn.bit_length() - 1):
        other_cache, other_fresh = from_partner((group_cache, group_fresh), "exp", bit)
        lower = position // (1 << bit) % 2 == 0
        group_cache = jnp.where(
            lower,
            jnp.concatenate([group_cache, other_cache], axis=1),
            jnp.concatenate([other_cache, group_cache], axis=1),
        )
        group_fresh = jnp.where(
            lower,
            jnp.concatenate([group_fresh, other_fresh], axis=1),
            jnp.concatenate([other_fresh, group_fresh], axis=1),
        )
    split_old = group_cache.reshape(cache_limit, heads_here, 2, head_dim)
    split_fresh = group_fresh.reshape(row_total, heads_here, 2, head_dim)
    attn_gates = pick_gates(group_normed, attn_router, group_routes)
    attn_tokens, attn_shares = slot_tables(
        group_routes, attn_gates, my_attn, rows_block, slot_count
    )
    token_flat = attn_tokens[:, 0, :].reshape(-1)
    share_flat = attn_shares[:, 0, :].reshape(-1)
    picked_rows = group_normed[token_flat]
    queries = jnp.einsum("sd,hdk->hsk", picked_rows, w_query, preferred_element_type=jnp.float32)
    queries = rotate(queries, (length + token_flat)[None, :]).astype(jnp.bfloat16)
    attend_heads = jax.vmap(attend, in_axes=(0, None, 1, 1, 1, 1, None))
    head_outs = attend_heads(
        queries,
        token_flat,
        split_old[:, :, 0],
        split_old[:, :, 1],
        split_fresh[:, :, 0],
        split_fresh[:, :, 1],
        length,
    )
    projected = jnp.einsum("hsk,hkd->sd", head_outs, w_out, preferred_element_type=jnp.float32)
    projected = (projected * share_flat[:, None]).reshape(block_count, slot_count, model_width)
    attn_ids = attn_tokens[:, 0, :]
    attn_own = lax.psum_scatter(
        spread_rows(projected, attn_ids, rows_block * lax.axis_size("exp")).astype(jnp.bfloat16),
        "exp",
        scatter_dimension=0,
        tiled=True,
    ).astype(jnp.float32)
    middle = lax.optimization_barrier(
        (own_rows.astype(jnp.float32) + attn_own).astype(jnp.bfloat16)
    )
    normed_mlp = rms_norm(middle, norm_mlp)
    experts_mlp = mlp_router.shape[1]
    split_count = device_count // experts_mlp
    my_expert = jnp.reshape(position // split_count, (1,))
    all_normed, all_routes = (
        lax.all_gather(normed_mlp, "exp", axis=0, tiled=True),
        lax.all_gather(mlp_routes[0], "exp", axis=0, tiled=True),
    )
    all_gates = pick_gates(all_normed, mlp_router, all_routes)
    mlp_tokens, mlp_shares = slot_tables(all_routes, all_gates, my_expert, rows_block, slot_count)
    inputs = all_normed[mlp_tokens.reshape(-1)]
    gate_part = jnp.dot(inputs, w_gate[0], preferred_element_type=jnp.float32)
    up_part = jnp.dot(inputs, w_up[0], preferred_element_type=jnp.float32)
    hidden = (jax.nn.silu(gate_part) * up_part).astype(jnp.bfloat16)
    slice_out = lax.optimization_barrier(
        jnp.dot(hidden, w_down[0], preferred_element_type=jnp.float32).astype(jnp.bfloat16)
    )
    weighted = (slice_out.astype(jnp.float32) * mlp_shares.reshape(-1)[:, None]).reshape(
        block_count, slot_count, model_width
    )
    mlp_ids = mlp_tokens[:, 0, :]
    mlp_own = lax.psum_scatter(
        spread_rows(weighted, mlp_ids, rows_block * lax.axis_size("exp")).astype(jnp.bfloat16),
        "exp",
        scatter_dimension=0,
        tiled=True,
    ).astype(jnp.float32)
    layer_out = (middle.astype(jnp.float32) + mlp_own).astype(jnp.bfloat16)
    return (layer_out[None], cache_next[None])


def solution(mesh):
    placed = (
        P("req", "exp", None),
        P("req", None, "exp"),
        P("req"),
        P("req", "exp", None),
        P("req", "exp", None),
        P(),
        P(),
        P("exp", None, None),
        P(None, "exp"),
        P("exp", None, None),
        P(),
        P(),
        P("exp", None, None),
        P("exp", None, None),
        P("exp", None, None),
    )
    return jax.shard_map(
        body,
        mesh=mesh,
        in_specs=placed,
        out_specs=(P("req", "exp", None), P("req", None, "exp")),
        check_vma=False,
    )
```

profile of v0, /device:TPU:0, one launch (start us, length us, event | category | flops | bytes accessed | tf_op | source)
XLA Modules:
  0.0 237.9 jit_solution(9046052581196760651)
XLA Ops:
  8.5 1.8 fusion.21
  11.3 15.7 %all_gather.7 = bf16[8,16,128]{2,1,0:T(8,128)(2,1)S(1)} all-gather(bf16[1,16,128]{2,1,0:T(8,128)(2,1)S(1)} %scatter.4), channel_id=1, replica_groups=mesh['req'=4,'exp'=8] {'exp'}, dimensions={0}, use_global_device_ids=true | all-gather | bytes 36864 | tf_op jit(solution)/shard_map/all_gather | solution.py:326
  38.7 3.6 %all-gather.2.cloned.1.call-done = bf16[512,2048]{1,0:T(8,128)(2,1)} async-done(((bf16[64,2048]{1,0:T(8,128)(2,1)}), bf16[512,2048]{1,0:T(8,128)(2,1)}) %all-gather.2.cloned.1.call-update) | async-done | bytes 2097168 | tf_op jit(solution)/shard_map/all_gather | solution.py:325
  42.3 2.9 %fusion.55 = f32[512,512]{0,1:T(8,128)S(1)} fusion(bf16[512,2048]{1,0:T(8,128)(2,1)} %all-gather.2.cloned.1.call-done, bf16[2048,512]{1,0:T(8,128)(2,1)S(1)} %copy-done), kind=kOutput, calls=%fused_computation.130 | convolution fusion | flops 1073741824 | bytes 5242880 | tf_op jit(solution)/shard_map/dot_general | solution.py:331
  45.3 6.3 %convolution_bitcast_fusion = f32[16,192,128]{2,1,0:T(8,128)S(1)} fusion(bf16[16,2048,128]{2,1,0:T(8,128)(2,1)} %param.26, bf16[512,2048]{1,0:T(8,128)(2,1)} %all-gather.2.cloned.1.call-done, s32[192]{0:T(256)S(1)} %bitcast.173), kind=kOutput, calls=%fused_computation.17 | convolution fusion | flops 2013757440 | bytes 12059392 | tf_op jit(solution)/shard_map/sd,hdk->hsk/dot_general | solution.py:352
  53.9 3.7 %all-to-all-start = ((bf16[8,2,192,128]{3,2,1,0:T(8,128)(2,1)}), bf16[8,2,192,128]{3,2,1,0:T(8,128)(2,1)S(1)}, u32[]{:S(2)}, u32[]{:S(2)}) async-start(bf16[8,2,192,128]{3,2,1,0:T(8,128)(2,1)} %bitcast.18), calls=%async_computation | async-start | bytes 1572864 | tf_op jit(solution)/shard_map/all_to_all | solution.py:357
  61.3 17.1 %all-to-all-done = bf16[8,2,192,128]{3,2,1,0:T(8,128)(2,1)S(1)} async-done(((bf16[8,2,192,128]{3,2,1,0:T(8,128)(2,1)}), bf16[8,2,192,128]{3,2,1,0:T(8,128)(2,1)S(1)}, u32[]{:S(2)}, u32[]{:S(2)}) %all-to-all-start) | async-done | bytes 786464 | tf_op jit(solution)/shard_map/all_to_all | solution.py:357
  79.4 9.0 %shard_map.158 = bf16[1,1536,128]{2,1,0:T(8,128)(2,1)} custom-call(s32[1]{0:T(128)} %copy.150.length_ref, bf16[1,1536,128]{2,1,0:T(8,128)(2,1)} %bitcast.162, s32[1536,1]{1,0:T(8,128)} %reshape_reshape_reshape.5.pos_ref, bf16[1,1536,128]{2,1,0:T(8,128)(2,1)} %get-tuple-element.28.key_ref, bf16[1,1536,128]{2,1,0:T(8,128)(2,1)} %get-tuple-element.26.value_ref), custom_call_target="tpu_custom_call" | custom-call | tf_op jit(solution)/shard_map/pallas_call | solution.py:260
  88.4 3.6 %all-to-all-start.1 = ((bf16[8,192,128]{2,1,0:T(8,128)(2,1)}), bf16[8,192,128]{2,1,0:T(8,128)(2,1)S(1)}, u32[]{:S(2)}, u32[]{:S(2)}) async-start(bf16[8,192,128]{2,1,0:T(8,128)(2,1)} %bitcast.160), calls=%async_computation.1 | async-start | bytes 786432 | tf_op jit(solution)/shard_map/all_to_all | solution.py:371
  92.2 9.0 %shard_map.159 = bf16[1,1536,128]{2,1,0:T(8,128)(2,1)} custom-call(s32[1]{0:T(128)} %copy.150.length_ref, bf16[1,1536,128]{2,1,0:T(8,128)(2,1)} %bitcast.159, s32[1536,1]{1,0:T(8,128)} %reshape_reshape_reshape.5.pos_ref, bf16[1,1536,128]{2,1,0:T(8,128)(2,1)} %get-tuple-element.27.key_ref, bf16[1,1536,128]{2,1,0:T(8,128)(2,1)} %get-tuple-element.25.value_ref), custom_call_target="tpu_custom_call" | custom-call | tf_op jit(solution)/shard_map/pallas_call | solution.py:260
  101.2 3.1 %all-to-all-done.1 = bf16[8,192,128]{2,1,0:T(8,128)(2,1)S(1)} async-done(((bf16[8,192,128]{2,1,0:T(8,128)(2,1)}), bf16[8,192,128]{2,1,0:T(8,128)(2,1)S(1)}, u32[]{:S(2)}, u32[]{:S(2)}) %all-to-all-start.1) | async-done | bytes 393248 | tf_op jit(solution)/shard_map/all_to_all | solution.py:371
  104.3 3.5 %all-to-all-start.2 = ((bf16[8,192,128]{2,1,0:T(8,128)(2,1)}), bf16[8,192,128]{2,1,0:T(8,128)(2,1)S(1)}, u32[]{:S(2)}, u32[]{:S(2)}) async-start(bf16[8,192,128]{2,1,0:T(8,128)(2,1)} %bitcast.161), calls=%async_computation.2 | async-start | bytes 786432 | tf_op jit(solution)/shard_map/all_to_all | solution.py:371
  107.9 4.4 %fusion.2 = f32[192,2048]{1,0:T(8,128)} fusion(bf16[8,192,128]{2,1,0:T(8,128)(2,1)S(1)} %all-to-all-done.1, bf16[8,2,128,2048]{3,2,1,0:T(8,128)(2,1)} %bitcast.174), kind=kOutput, calls=%fused_computation.6 | convolution fusion | flops 805306368 | bytes 6160384 | tf_op jit(solution)/shard_map/dsk,dkm->sm/dot_general | solution.py:374
  112.3 7.9 %all-to-all-done.2 = bf16[8,192,128]{2,1,0:T(8,128)(2,1)S(1)} async-done(((bf16[8,192,128]{2,1,0:T(8,128)(2,1)}), bf16[8,192,128]{2,1,0:T(8,128)(2,1)S(1)}, u32[]{:S(2)}, u32[]{:S(2)}) %all-to-all-start.2) | async-done | bytes 393248 | tf_op jit(solution)/shard_map/all_to_all | solution.py:371
  120.3 4.6 %fusion.5 = bf16[192,2048]{1,0:T(8,128)(2,1)} fusion(f32[192,2048]{1,0:T(8,128)} %fusion.2, bf16[8,192,128]{2,1,0:T(8,128)(2,1)S(1)} %all-to-all-done.2, bf16[8,2,128,2048]{3,2,1,0:T(8,128)(2,1)} %bitcast.175), kind=kOutput, calls=%fused_computation.9 | convolution fusion | flops 806092800 | bytes 6946816 | tf_op jit(solution)/shard_map/dsk,dkm->sm/dot_general | solution.py:374
  124.9 3.5 %all-to-all-start.3 = ((bf16[8,24,2048]{2,1,0:T(8,128)(2,1)}), bf16[8,24,2048]{2,1,0:T(8,128)(2,1)S(1)}, u32[]{:S(2)}, u32[]{:S(2)}) async-start(bf16[8,24,2048]{2,1,0:T(8,128)(2,1)} %bitcast.39), calls=%async_computation.3 | async-start | bytes 1572864 | tf_op jit(solution)/shard_map/all_to_all | solution.py:378
  130.6 18.8 %all-to-all-done.3 = bf16[8,24,2048]{2,1,0:T(8,128)(2,1)S(1)} async-done(((bf16[8,24,2048]{2,1,0:T(8,128)(2,1)}), bf16[8,24,2048]{2,1,0:T(8,128)(2,1)S(1)}, u32[]{:S(2)}, u32[]{:S(2)}) %all-to-all-start.3) | async-done | bytes 786464 | tf_op jit(solution)/shard_map/all_to_all | solution.py:378
  151.7 3.5 %all-to-all-start.4 = ((bf16[8,24,2048]{2,1,0:T(8,128)(2,1)}), bf16[8,24,2048]{2,1,0:T(8,128)(2,1)S(1)}, u32[]{:S(2)}, u32[]{:S(2)}) async-start(bf16[8,24,2048]{2,1,0:T(8,128)(2,1)} %bitcast.47), calls=%async_computation.4 | async-start | bytes 1572864 | tf_op jit(solution)/shard_map/all_to_all | solution.py:397
  157.3 3.1 %dynamic_update_slice.3 = bf16[1536,512]{1,0:T(8,128)(2,1)S(1)} dynamic-update-slice(bf16[1536,512]{1,0:T(8,128)(2,1)S(1)} %broadcast_in_dim.18, bf16[512,512]{1,0:T(8,128)(2,1)S(1)} %copy.140, s32[]{:T(128)S(6)} %select_n.17, s32[]{:T(128)} %constant.74.clone.1) | dynamic-update-slice | bytes 1048580 | tf_op jit(solution)/shard_map/dynamic_update_slice | solution.py:341
  160.3 15.8 %all-to-all-done.4 = bf16[8,24,2048]{2,1,0:T(8,128)(2,1)S(1)} async-done(((bf16[8,24,2048]{2,1,0:T(8,128)(2,1)}), bf16[8,24,2048]{2,1,0:T(8,128)(2,1)S(1)}, u32[]{:S(2)}, u32[]{:S(2)}) %all-to-all-start.4) | async-done | bytes 786464 | tf_op jit(solution)/shard_map/all_to_all | solution.py:397
  177.0 28.0 %shard_map.160 = bf16[192,2048]{1,0:T(8,128)(2,1)} custom-call(bf16[192,2048]{1,0:T(8,128)(2,1)} %bitcast.153, bf16[1,2048,5632]{2,1,0:T(8,128)(2,1)} %gate_ref.1, bf16[1,2048,5632]{2,1,0:T(8,128)(2,1)} %up_ref.1, bf16[1,5632,2048]{2,1,0:T(8,128)(2,1)} %down_ref.1), custom_call_target="tpu_custom_call" | custom-call | tf_op jit(solution)/shard_map/pallas_call | solution.py:206
  205.0 3.5 %all-to-all-start.5 = ((bf16[8,24,2048]{2,1,0:T(8,128)(2,1)}), bf16[8,24,2048]{2,1,0:T(8,128)(2,1)S(1)}, u32[]{:S(2)}, u32[]{:S(2)}) async-start(bf16[8,24,2048]{2,1,0:T(8,128)(2,1)} %bitcast.154), calls=%async_computation.5 | async-start | bytes 1572864 | tf_op jit(solution)/shard_map/all_to_all | solution.py:399
  208.6 2.9 %select_bitcast_fusion = bf16[1,1536,512]{2,1,0:T(8,128)(2,1)} fusion(bf16[1536,512]{1,0:T(8,128)(2,1)S(1)} %dynamic_update_slice.3, bf16[1024,512]{1,0:T(8,128)(2,1)} %bitcast.152, pred[1536]{0:T(1024)(128)(4,1)S(1)} %iota_compare_fusion.20), kind=kLoop, calls=%fused_computation.16 | loop fusion | flops 786432 | bytes 4195840 | tf_op jit(solution)/shard_map/broadcast_in_dim | solution.py:406
  211.8 17.7 %all-to-all-done.5 = bf16[8,24,2048]{2,1,0:T(8,128)(2,1)S(1)} async-done(((bf16[8,24,2048]{2,1,0:T(8,128)(2,1)}), bf16[8,24,2048]{2,1,0:T(8,128)(2,1)S(1)}, u32[]{:S(2)}, u32[]{:S(2)}) %all-to-all-start.5) | async-done | bytes 786464 | tf_op jit(solution)/shard_map/all_to_all | solution.py:399
  (116 shorter events, 29.7 us)
Async XLA Ops:
  7.2 35.2 %copy-start = (bf16[2048,512]{1,0:T(8,128)(2,1)S(1)}, bf16[2048,512]{1,0:T(8,128)(2,1)}, u32[]{:S(2)}) copy-start(bf16[2048,512]{1,0:T(8,128)(2,1)} %param.27) | copy-start | bytes 6291460
  7.2 35.1 %all-gather.2.cloned.1.call-start = ((), (), s32[]{:S(2)}) async-start(), calls=%async_computation.6 | async-start | bytes 2359296 | tf_op jit(solution)/shard_map/all_gather | solution.py:325
  51.6 0.9 copy-start.6
  53.9 4.1 %copy-start.5 = (f32[512,64]{1,0:T(8,128)S(1)}, f32[512,64]{1,0:T(8,128)}, u32[]{:S(2)}) copy-start(f32[512,64]{1,0:T(8,128)} %get-tuple-element.33) | copy-start | bytes 393220
  53.9 24.6 %all-to-all-start = ((bf16[8,2,192,128]{3,2,1,0:T(8,128)(2,1)}), bf16[8,2,192,128]{3,2,1,0:T(8,128)(2,1)S(1)}, u32[]{:S(2)}, u32[]{:S(2)}) async-start(bf16[8,2,192,128]{3,2,1,0:T(8,128)(2,1)} %bitcast.18), calls=%async_computation | async-start | bytes 1572864 | tf_op jit(solution)/shard_map/all_to_all | solution.py:357
  79.4 12.7 %copy-start.9 = (s32[1,64,2]{1,2,0:T(2,128)S(1)}, s32[1,64,2]{1,2,0:T(2,128)}, u32[]{:S(2)}) copy-start(s32[1,64,2]{1,2,0:T(2,128)} %param.23) | copy-start | bytes 1540
  79.4 12.7 %copy-start.8 = (s32[1,64,2]{1,2,0:T(2,128)S(1)}, s32[1,64,2]{1,2,0:T(2,128)}, u32[]{:S(2)}) copy-start(s32[1,64,2]{1,2,0:T(2,128)} %param.22) | copy-start | bytes 1540
  88.4 15.9 %all-to-all-start.1 = ((bf16[8,192,128]{2,1,0:T(8,128)(2,1)}), bf16[8,192,128]{2,1,0:T(8,128)(2,1)S(1)}, u32[]{:S(2)}, u32[]{:S(2)}) async-start(bf16[8,192,128]{2,1,0:T(8,128)(2,1)} %bitcast.160), calls=%async_computation.1 | async-start | bytes 786432 | tf_op jit(solution)/shard_map/all_to_all | solution.py:371
  104.3 15.9 %all-to-all-start.2 = ((bf16[8,192,128]{2,1,0:T(8,128)(2,1)}), bf16[8,192,128]{2,1,0:T(8,128)(2,1)S(1)}, u32[]{:S(2)}, u32[]{:S(2)}) async-start(bf16[8,192,128]{2,1,0:T(8,128)(2,1)} %bitcast.161), calls=%async_computation.2 | async-start | bytes 786432 | tf_op jit(solution)/shard_map/all_to_all | solution.py:371
  124.9 24.4 %all-to-all-start.3 = ((bf16[8,24,2048]{2,1,0:T(8,128)(2,1)}), bf16[8,24,2048]{2,1,0:T(8,128)(2,1)S(1)}, u32[]{:S(2)}, u32[]{:S(2)}) async-start(bf16[8,24,2048]{2,1,0:T(8,128)(2,1)} %bitcast.39), calls=%async_computation.3 | async-start | bytes 1572864 | tf_op jit(solution)/shard_map/all_to_all | solution.py:378
  128.9 1.4 copy-start.4
  128.9 1.4 copy-start.7
  129.9 20.0 %copy-start.3 = (bf16[1,64,2048]{2,1,0:T(8,128)(2,1)S(1)}, bf16[1,64,2048]{2,1,0:T(8,128)(2,1)}, u32[]{:S(2)}) copy-start(bf16[1,64,2048]{2,1,0:T(8,128)(2,1)} %param.19) | copy-start | bytes 786436
  149.6 0.7 copy-start.10
  151.7 24.5 %all-to-all-start.4 = ((bf16[8,24,2048]{2,1,0:T(8,128)(2,1)}), bf16[8,24,2048]{2,1,0:T(8,128)(2,1)S(1)}, u32[]{:S(2)}, u32[]{:S(2)}) async-start(bf16[8,24,2048]{2,1,0:T(8,128)(2,1)} %bitcast.47), calls=%async_computation.4 | async-start | bytes 1572864 | tf_op jit(solution)/shard_map/all_to_all | solution.py:397
  176.1 0.9 copy-start.2
  205.0 24.4 %all-to-all-start.5 = ((bf16[8,24,2048]{2,1,0:T(8,128)(2,1)}), bf16[8,24,2048]{2,1,0:T(8,128)(2,1)S(1)}, u32[]{:S(2)}, u32[]{:S(2)}) async-start(bf16[8,24,2048]{2,1,0:T(8,128)(2,1)} %bitcast.154), calls=%async_computation.5 | async-start | bytes 1572864 | tf_op jit(solution)/shard_map/all_to_all | solution.py:399
  208.6 2.9 %copy-start.11 = (bf16[2048,8]{0,1:T(8,128)(2,1)S(1)}, bf16[2048,8]{0,1:T(8,128)(2,1)}, u32[]{:S(2)}) copy-start(bf16[2048,8]{0,1:T(8,128)(2,1)} %param.30) | copy-start | bytes 98308
  229.5 1.6 copy-start.1
Sparse Core Ops, SparseCore 0:
  10.4 31.8 all-gather.1
where the time goes:
time: 239 us; the launch traced here: 238 us
  waiting for transfers between devices  84 us (35%)
  Pallas kernels  46 us (19%)
  matrix products  21.5 us (9%)
  starting transfers between devices  21.4 us (9%)
  local copies, waits for them, and re-layouts  18.7 us (8%)
  blocking collectives  15.7 us (7%)
  other arithmetic  15.4 us (6%)
  between operations  15.2 us (6%)
    pallas_call x1, Pallas kernels, expert_mlp(): pl.pallas_call(mlp_kernel, grid=(hidden_units // tile,), in_specs=[pl.Blo...  28 us
    all_to_all x1, waiting for transfers between devices, body(): recv_p = lax.all_to_all(send_p, 'exp', 0, 0, tiled=True)  18.8 us
    pallas_call x2, Pallas kernels, kernel_attention(): pl.pallas_call(functools.partial(attention_kernel, cache_limit=cache_limi...  18 us
    all_to_all x1, waiting for transfers between devices, body(): lax.all_to_all(slice_out.reshape(device_count, slot_count, model_width),...  17.7 us
    all_to_all x1, waiting for transfers between devices, body(): recv_q = lax.all_to_all(send_q, 'exp', 0, 0, tiled=True)  17.1 us
    all_to_all x1, waiting for transfers between devices, body(): lax.all_to_all(send_m, 'exp', 0, 0, tiled=True).reshape(-1, model_width)  15.8 us
    all_gather x1, blocking collectives, body(): gathered_routes = lax.all_gather(route_rows, 'exp', axis=0, tiled=False)  15.7 us
    all_to_all x2, waiting for transfers between devices, body(): lax.all_to_all(head_out.reshape(device_count, query_slots, head_dim), 'ex...  11 us
  transfers between devices with their start and end apart: 7, of which 7 were waited for; matrix products, arithmetic and copies ran while one was open for 13% of the time, Pallas kernels for 4%

commit v1 on v0

--- a/solution.py
+++ b/solution.py
@@ -245,7 +245,7 @@
 def kernel_attention(queries, query_pos, keys, values, length, cache_limit):
     head_count, query_count, head_dim = queries.shape
     key_count = keys.shape[1]
-    tile = next(t for t in (512, 256, 128, 64, 32, 16, 8) if query_count % t == 0)
+    tile = next(t for t in (384, 256, 128, 64, 32, 16, 8) if query_count % t == 0)
     grid_spec = pltpu.PrefetchScalarGridSpec(
         num_scalar_prefetch=1,
         grid=(head_count, query_count // tile),

time: 239 us -> 239 us (level)
  no operation moved by 1% of the time
where the time goes in v1:
time: 239 us; the launch traced here: 238 us
  waiting for transfers between devices  83.7 us (35%)
  Pallas kernels  46.6 us (19%)
  matrix products  21.5 us (9%)
  starting transfers between devices  21.4 us (9%)
  local copies, waits for them, and re-layouts  18.7 us (8%)
  blocking collectives  15.7 us (7%)
  other arithmetic  15.4 us (6%)
  between operations  15.2 us (6%)
    pallas_call x1, Pallas kernels, expert_mlp(): pl.pallas_call(mlp_kernel, grid=(hidden_units // tile,), in_specs=[pl.Blo...  28 us
    all_to_all x1, waiting for transfers between devices, body(): recv_p = lax.all_to_all(send_p, 'exp', 0, 0, tiled=True)  18.8 us
    pallas_call x2, Pallas kernels, kernel_attention(): pl.pallas_call(functools.partial(attention_kernel, cache_limit=cache_limi...  18.5 us
    all_to_all x1, waiting for transfers between devices, body(): lax.all_to_all(slice_out.reshape(device_count, slot_count, model_width),...  17.7 us
    all_to_all x1, waiting for transfers between devices, body(): recv_q = lax.all_to_all(send_q, 'exp', 0, 0, tiled=True)  17.1 us
    all_to_all x1, waiting for transfers between devices, body(): lax.all_to_all(send_m, 'exp', 0, 0, tiled=True).reshape(-1, model_width)  15.8 us
    all_gather x1, blocking collectives, body(): gathered_routes = lax.all_gather(route_rows, 'exp', axis=0, tiled=False)  15.7 us
    all_to_all x2, waiting for transfers between devices, body(): lax.all_to_all(head_out.reshape(device_count, query_slots, head_dim), 'ex...  10.8 us
  transfers between devices with their start and end apart: 7, of which 7 were waited for; matrix products, arithmetic and copies ran while one was open for 13% of the time, Pallas kernels for 4%

profile of v1, /device:TPU:0, one launch (start us, length us, event | category | flops | bytes accessed | tf_op | source)
XLA Modules:
  0.0 238.2 jit_solution(531526079637201142)
XLA Ops:
  8.5 1.8 fusion.21
  11.3 15.7 %all_gather.7 = bf16[8,16,128]{2,1,0:T(8,128)(2,1)S(1)} all-gather(bf16[1,16,128]{2,1,0:T(8,128)(2,1)S(1)} %scatter.4), channel_id=1, replica_groups=mesh['req'=4,'exp'=8] {'exp'}, dimensions={0}, use_global_device_ids=true | all-gather | bytes 36864 | tf_op jit(solution)/shard_map/all_gather | solution.py:326
  38.7 3.6 %all-gather.2.cloned.1.call-done = bf16[512,2048]{1,0:T(8,128)(2,1)} async-done(((bf16[64,2048]{1,0:T(8,128)(2,1)}), bf16[512,2048]{1,0:T(8,128)(2,1)}) %all-gather.2.cloned.1.call-update) | async-done | bytes 2097168 | tf_op jit(solution)/shard_map/all_gather | solution.py:325
  42.3 2.9 %fusion.55 = f32[512,512]{0,1:T(8,128)S(1)} fusion(bf16[512,2048]{1,0:T(8,128)(2,1)} %all-gather.2.cloned.1.call-done, bf16[2048,512]{1,0:T(8,128)(2,1)S(1)} %copy-done), kind=kOutput, calls=%fused_computation.130 | convolution fusion | flops 1073741824 | bytes 5242880 | tf_op jit(solution)/shard_map/dot_general | solution.py:331
  45.3 6.3 %convolution_bitcast_fusion = f32[16,192,128]{2,1,0:T(8,128)S(1)} fusion(bf16[16,2048,128]{2,1,0:T(8,128)(2,1)} %param.26, bf16[512,2048]{1,0:T(8,128)(2,1)} %all-gather.2.cloned.1.call-done, s32[192]{0:T(256)S(1)} %bitcast.173), kind=kOutput, calls=%fused_computation.17 | convolution fusion | flops 2013757440 | bytes 12059392 | tf_op jit(solution)/shard_map/sd,hdk->hsk/dot_general | solution.py:352
  53.9 3.7 %all-to-all-start = ((bf16[8,2,192,128]{3,2,1,0:T(8,128)(2,1)}), bf16[8,2,192,128]{3,2,1,0:T(8,128)(2,1)S(1)}, u32[]{:S(2)}, u32[]{:S(2)}) async-start(bf16[8,2,192,128]{3,2,1,0:T(8,128)(2,1)} %bitcast.18), calls=%async_computation | async-start | bytes 1572864 | tf_op jit(solution)/shard_map/all_to_all | solution.py:357
  61.3 17.1 %all-to-all-done = bf16[8,2,192,128]{3,2,1,0:T(8,128)(2,1)S(1)} async-done(((bf16[8,2,192,128]{3,2,1,0:T(8,128)(2,1)}), bf16[8,2,192,128]{3,2,1,0:T(8,128)(2,1)S(1)}, u32[]{:S(2)}, u32[]{:S(2)}) %all-to-all-start) | async-done | bytes 786464 | tf_op jit(solution)/shard_map/all_to_all | solution.py:357
  79.4 9.3 %shard_map.158 = bf16[1,1536,128]{2,1,0:T(8,128)(2,1)} custom-call(s32[1]{0:T(128)} %copy.150.length_ref, bf16[1,1536,128]{2,1,0:T(8,128)(2,1)} %bitcast.162, s32[1536,1]{1,0:T(8,128)} %reshape_reshape_reshape.5.pos_ref, bf16[1,1536,128]{2,1,0:T(8,128)(2,1)} %get-tuple-element.28.key_ref, bf16[1,1536,128]{2,1,0:T(8,128)(2,1)} %get-tuple-element.26.value_ref), custom_call_target="tpu_custom_call" | custom-call | tf_op jit(solution)/shard_map/pallas_call | solution.py:260
  88.7 3.6 %all-to-all-start.1 = ((bf16[8,192,128]{2,1,0:T(8,128)(2,1)}), bf16[8,192,128]{2,1,0:T(8,128)(2,1)S(1)}, u32[]{:S(2)}, u32[]{:S(2)}) async-start(bf16[8,192,128]{2,1,0:T(8,128)(2,1)} %bitcast.160), calls=%async_computation.1 | async-start | bytes 786432 | tf_op jit(solution)/shard_map/all_to_all | solution.py:371
  92.5 9.3 %shard_map.159 = bf16[1,1536,128]{2,1,0:T(8,128)(2,1)} custom-call(s32[1]{0:T(128)} %copy.150.length_ref, bf16[1,1536,128]{2,1,0:T(8,128)(2,1)} %bitcast.159, s32[1536,1]{1,0:T(8,128)} %reshape_reshape_reshape.5.pos_ref, bf16[1,1536,128]{2,1,0:T(8,128)(2,1)} %get-tuple-element.27.key_ref, bf16[1,1536,128]{2,1,0:T(8,128)(2,1)} %get-tuple-element.25.value_ref), custom_call_target="tpu_custom_call" | custom-call | tf_op jit(solution)/shard_map/pallas_call | solution.py:260
  101.8 2.8 %all-to-all-done.1 = bf16[8,192,128]{2,1,0:T(8,128)(2,1)S(1)} async-done(((bf16[8,192,128]{2,1,0:T(8,128)(2,1)}), bf16[8,192,128]{2,1,0:T(8,128)(2,1)S(1)}, u32[]{:S(2)}, u32[]{:S(2)}) %all-to-all-start.1) | async-done | bytes 393248 | tf_op jit(solution)/shard_map/all_to_all | solution.py:371
  104.6 3.5 %all-to-all-start.2 = ((bf16[8,192,128]{2,1,0:T(8,128)(2,1)}), bf16[8,192,128]{2,1,0:T(8,128)(2,1)S(1)}, u32[]{:S(2)}, u32[]{:S(2)}) async-start(bf16[8,192,128]{2,1,0:T(8,128)(2,1)} %bitcast.161), calls=%async_computation.2 | async-start | bytes 786432 | tf_op jit(solution)/shard_map/all_to_all | solution.py:371
  108.2 4.4 %fusion.2 = f32[192,2048]{1,0:T(8,128)} fusion(bf16[8,192,128]{2,1,0:T(8,128)(2,1)S(1)} %all-to-all-done.1, bf16[8,2,128,2048]{3,2,1,0:T(8,128)(2,1)} %bitcast.174), kind=kOutput, calls=%fused_computation.6 | convolution fusion | flops 805306368 | bytes 6160384 | tf_op jit(solution)/shard_map/dsk,dkm->sm/dot_general | solution.py:374
  112.6 7.9 %all-to-all-done.2 = bf16[8,192,128]{2,1,0:T(8,128)(2,1)S(1)} async-done(((bf16[8,192,128]{2,1,0:T(8,128)(2,1)}), bf16[8,192,128]{2,1,0:T(8,128)(2,1)S(1)}, u32[]{:S(2)}, u32[]{:S(2)}) %all-to-all-start.2) | async-done | bytes 393248 | tf_op jit(solution)/shard_map/all_to_all | solution.py:371
  120.5 4.6 %fusion.5 = bf16[192,2048]{1,0:T(8,128)(2,1)} fusion(f32[192,2048]{1,0:T(8,128)} %fusion.2, bf16[8,192,128]{2,1,0:T(8,128)(2,1)S(1)} %all-to-all-done.2, bf16[8,2,128,2048]{3,2,1,0:T(8,128)(2,1)} %bitcast.175), kind=kOutput, calls=%fused_computation.9 | convolution fusion | flops 806092800 | bytes 6946816 | tf_op jit(solution)/shard_map/dsk,dkm->sm/dot_general | solution.py:374
  125.2 3.5 %all-to-all-start.3 = ((bf16[8,24,2048]{2,1,0:T(8,128)(2,1)}), bf16[8,24,2048]{2,1,0:T(8,128)(2,1)S(1)}, u32[]{:S(2)}, u32[]{:S(2)}) async-start(bf16[8,24,2048]{2,1,0:T(8,128)(2,1)} %bitcast.39), calls=%async_computation.3 | async-start | bytes 1572864 | tf_op jit(solution)/shard_map/all_to_all | solution.py:378
  130.9 18.8 %all-to-all-done.3 = bf16[8,24,2048]{2,1,0:T(8,128)(2,1)S(1)} async-done(((bf16[8,24,2048]{2,1,0:T(8,128)(2,1)}), bf16[8,24,2048]{2,1,0:T(8,128)(2,1)S(1)}, u32[]{:S(2)}, u32[]{:S(2)}) %all-to-all-start.3) | async-done | bytes 786464 | tf_op jit(solution)/shard_map/all_to_all | solution.py:378
  151.9 3.5 %all-to-all-start.4 = ((bf16[8,24,2048]{2,1,0:T(8,128)(2,1)}), bf16[8,24,2048]{2,1,0:T(8,128)(2,1)S(1)}, u32[]{:S(2)}, u32[]{:S(2)}) async-start(bf16[8,24,2048]{2,1,0:T(8,128)(2,1)} %bitcast.47), calls=%async_computation.4 | async-start | bytes 1572864 | tf_op jit(solution)/shard_map/all_to_all | solution.py:397
  157.6 3.1 %dynamic_update_slice.3 = bf16[1536,512]{1,0:T(8,128)(2,1)S(1)} dynamic-update-slice(bf16[1536,512]{1,0:T(8,128)(2,1)S(1)} %broadcast_in_dim.18, bf16[512,512]{1,0:T(8,128)(2,1)S(1)} %copy.140, s32[]{:T(128)S(6)} %select_n.17, s32[]{:T(128)} %constant.74.clone.1) | dynamic-update-slice | bytes 1048580 | tf_op jit(solution)/shard_map/dynamic_update_slice | solution.py:341
  160.6 15.8 %all-to-all-done.4 = bf16[8,24,2048]{2,1,0:T(8,128)(2,1)S(1)} async-done(((bf16[8,24,2048]{2,1,0:T(8,128)(2,1)}), bf16[8,24,2048]{2,1,0:T(8,128)(2,1)S(1)}, u32[]{:S(2)}, u32[]{:S(2)}) %all-to-all-start.4) | async-done | bytes 786464 | tf_op jit(solution)/shard_map/all_to_all | solution.py:397
  177.3 28.0 %shard_map.160 = bf16[192,2048]{1,0:T(8,128)(2,1)} custom-call(bf16[192,2048]{1,0:T(8,128)(2,1)} %bitcast.153, bf16[1,2048,5632]{2,1,0:T(8,128)(2,1)} %gate_ref.1, bf16[1,2048,5632]{2,1,0:T(8,128)(2,1)} %up_ref.1, bf16[1,5632,2048]{2,1,0:T(8,128)(2,1)} %down_ref.1), custom_call_target="tpu_custom_call" | custom-call | tf_op jit(solution)/shard_map/pallas_call | solution.py:206
  205.3 3.5 %all-to-all-start.5 = ((bf16[8,24,2048]{2,1,0:T(8,128)(2,1)}), bf16[8,24,2048]{2,1,0:T(8,128)(2,1)S(1)}, u32[]{:S(2)}, u32[]{:S(2)}) async-start(bf16[8,24,2048]{2,1,0:T(8,128)(2,1)} %bitcast.154), calls=%async_computation.5 | async-start | bytes 1572864 | tf_op jit(solution)/shard_map/all_to_all | solution.py:399
  208.9 2.9 %select_bitcast_fusion = bf16[1,1536,512]{2,1,0:T(8,128)(2,1)} fusion(bf16[1536,512]{1,0:T(8,128)(2,1)S(1)} %dynamic_update_slice.3, bf16[1024,512]{1,0:T(8,128)(2,1)} %bitcast.152, pred[1536]{0:T(1024)(128)(4,1)S(1)} %iota_compare_fusion.20), kind=kLoop, calls=%fused_computation.16 | loop fusion | flops 786432 | bytes 4195840 | tf_op jit(solution)/shard_map/broadcast_in_dim | solution.py:406
  212.1 17.7 %all-to-all-done.5 = bf16[8,24,2048]{2,1,0:T(8,128)(2,1)S(1)} async-done(((bf16[8,24,2048]{2,1,0:T(8,128)(2,1)}), bf16[8,24,2048]{2,1,0:T(8,128)(2,1)S(1)}, u32[]{:S(2)}, u32[]{:S(2)}) %all-to-all-start.5) | async-done | bytes 786464 | tf_op jit(solution)/shard_map/all_to_all | solution.py:399
  (116 shorter events, 29.7 us)
Async XLA Ops:
  7.2 35.2 %copy-start = (bf16[2048,512]{1,0:T(8,128)(2,1)S(1)}, bf16[2048,512]{1,0:T(8,128)(2,1)}, u32[]{:S(2)}) copy-start(bf16[2048,512]{1,0:T(8,128)(2,1)} %param.27) | copy-start | bytes 6291460
  7.2 35.1 %all-gather.2.cloned.1.call-start = ((), (), s32[]{:S(2)}) async-start(), calls=%async_computation.6 | async-start | bytes 2359296 | tf_op jit(solution)/shard_map/all_gather | solution.py:325
  51.6 0.9 copy-start.6
  53.9 4.1 %copy-start.5 = (f32[512,64]{1,0:T(8,128)S(1)}, f32[512,64]{1,0:T(8,128)}, u32[]{:S(2)}) copy-start(f32[512,64]{1,0:T(8,128)} %get-tuple-element.33) | copy-start | bytes 393220
  53.9 24.6 %all-to-all-start = ((bf16[8,2,192,128]{3,2,1,0:T(8,128)(2,1)}), bf16[8,2,192,128]{3,2,1,0:T(8,128)(2,1)S(1)}, u32[]{:S(2)}, u32[]{:S(2)}) async-start(bf16[8,2,192,128]{3,2,1,0:T(8,128)(2,1)} %bitcast.18), calls=%async_computation | async-start | bytes 1572864 | tf_op jit(solution)/shard_map/all_to_all | solution.py:357
  79.4 12.9 %copy-start.9 = (s32[1,64,2]{1,2,0:T(2,128)S(1)}, s32[1,64,2]{1,2,0:T(2,128)}, u32[]{:S(2)}) copy-start(s32[1,64,2]{1,2,0:T(2,128)} %param.23) | copy-start | bytes 1540
  79.4 13.0 %copy-start.8 = (s32[1,64,2]{1,2,0:T(2,128)S(1)}, s32[1,64,2]{1,2,0:T(2,128)}, u32[]{:S(2)}) copy-start(s32[1,64,2]{1,2,0:T(2,128)} %param.22) | copy-start | bytes 1540
  88.7 15.9 %all-to-all-start.1 = ((bf16[8,192,128]{2,1,0:T(8,128)(2,1)}), bf16[8,192,128]{2,1,0:T(8,128)(2,1)S(1)}, u32[]{:S(2)}, u32[]{:S(2)}) async-start(bf16[8,192,128]{2,1,0:T(8,128)(2,1)} %bitcast.160), calls=%async_computation.1 | async-start | bytes 786432 | tf_op jit(solution)/shard_map/all_to_all | solution.py:371
  104.6 15.9 %all-to-all-start.2 = ((bf16[8,192,128]{2,1,0:T(8,128)(2,1)}), bf16[8,192,128]{2,1,0:T(8,128)(2,1)S(1)}, u32[]{:S(2)}, u32[]{:S(2)}) async-start(bf16[8,192,128]{2,1,0:T(8,128)(2,1)} %bitcast.161), calls=%async_computation.2 | async-start | bytes 786432 | tf_op jit(solution)/shard_map/all_to_all | solution.py:371
  125.2 24.4 %all-to-all-start.3 = ((bf16[8,24,2048]{2,1,0:T(8,128)(2,1)}), bf16[8,24,2048]{2,1,0:T(8,128)(2,1)S(1)}, u32[]{:S(2)}, u32[]{:S(2)}) async-start(bf16[8,24,2048]{2,1,0:T(8,128)(2,1)} %bitcast.39), calls=%async_computation.3 | async-start | bytes 1572864 | tf_op jit(solution)/shard_map/all_to_all | solution.py:378
  129.2 1.4 copy-start.4
  129.2 1.4 copy-start.7
  130.2 20.0 %copy-start.3 = (bf16[1,64,2048]{2,1,0:T(8,128)(2,1)S(1)}, bf16[1,64,2048]{2,1,0:T(8,128)(2,1)}, u32[]{:S(2)}) copy-start(bf16[1,64,2048]{2,1,0:T(8,128)(2,1)} %param.19) | copy-start | bytes 786436
  149.9 0.7 copy-start.10
  151.9 24.5 %all-to-all-start.4 = ((bf16[8,24,2048]{2,1,0:T(8,128)(2,1)}), bf16[8,24,2048]{2,1,0:T(8,128)(2,1)S(1)}, u32[]{:S(2)}, u32[]{:S(2)}) async-start(bf16[8,24,2048]{2,1,0:T(8,128)(2,1)} %bitcast.47), calls=%async_computation.4 | async-start | bytes 1572864 | tf_op jit(solution)/shard_map/all_to_all | solution.py:397
  176.4 0.9 copy-start.2
  205.3 24.4 %all-to-all-start.5 = ((bf16[8,24,2048]{2,1,0:T(8,128)(2,1)}), bf16[8,24,2048]{2,1,0:T(8,128)(2,1)S(1)}, u32[]{:S(2)}, u32[]{:S(2)}) async-start(bf16[8,24,2048]{2,1,0:T(8,128)(2,1)} %bitcast.154), calls=%async_computation.5 | async-start | bytes 1572864 | tf_op jit(solution)/shard_map/all_to_all | solution.py:399
  208.8 2.9 %copy-start.11 = (bf16[2048,8]{0,1:T(8,128)(2,1)S(1)}, bf16[2048,8]{0,1:T(8,128)(2,1)}, u32[]{:S(2)}) copy-start(bf16[2048,8]{0,1:T(8,128)(2,1)} %param.30) | copy-start | bytes 98308
  229.7 1.6 copy-start.1
Sparse Core Ops, SparseCore 0:
  10.4 31.8 all-gather.1
